TPU v7x, 32 devices: a whole 2x2x4 slice. The times are simulated.
32 devices in a mesh: dp: 4 (over z), fsdp: 2 (over x), rows: 4 (over y, core).
Axes of the slice: x: 2, y: 2, z: 4, core: 2. Of those that a mesh axis runs over, the one named last changes fastest.
Arguments:
- feature_maps: bfloat16 [8, 16, 32, 1536], P(('dp', 'fsdp'), 'rows'), may hold values from -30 to 30
- dw_kernel: float32 [7, 7, 1536], replicated, may hold values from -0.875 to 0.875
- norm_gain: float32 [1536], replicated, may hold values from 0.5 to 1.5
- w_up: bfloat16 [1536, 6144], P(('dp', 'rows'), 'fsdp'), may hold values from -0.15625 to 0.15625
- w_down: bfloat16 [6144, 1536], P('fsdp', ('dp', 'rows')), may hold values from -0.078125 to 0.078125
- layer_scale: float32 [1536], replicated, may hold values from 0.3 to 1.5
- d_out: bfloat16 [8, 16, 32, 1536], P(('dp', 'fsdp'), 'rows'), may hold values from -20 to 20
Outputs:
- result: bfloat16 [8, 16, 32, 1536], P(('dp', 'fsdp'), 'rows')
- grad_x: bfloat16 [8, 16, 32, 1536], P(('dp', 'fsdp'), 'rows')
- grad_up: float32 [1536, 6144], P(('dp', 'rows'), 'fsdp')
- grad_down: float32 [6144, 1536], P('fsdp', ('dp', 'rows'))
- grad_kernel: float32 [7, 7, 1536], replicated
- grad_gain: float32 [1536], replicated
- grad_scale: float32 [1536], replicated
All inputs are finite; a program needn't handle non-finite values.
Results may differ from a plain program's by a relative error of at most 0.0075.
Values may be sent and summed in bfloat16 or wider, within the bound.
No kernel may reach another device: no remote copies, remote signals or barrier semaphores. Data moves between devices by JAX's collectives and lax.ppermute only.
A program may use at most 128 MiB of HBM per device.

v0:
```python
import math
import jax
import jax.numpy as jnp
from jax import lax
from jax.sharding import PartitionSpec as P

KS = 7
norm_eps = 1e-06
inv_root_two = 1.0 / math.sqrt(2.0)
inv_root_two_pi = 1.0 / math.sqrt(2.0 * math.pi)
contract_rows = (((0,), (0,)), ((), ()))
contract_cols = (((1,), (1,)), ((), ()))


def padded_2(x, sides, width):
    for axis, dim in sides:
        devices, length = (lax.axis_size(axis), x.shape[dim])
        up = [(i, (i + 1) % devices) for i in range(devices - 1)]
        down = [(j, i) for i, j in up]
        last = lax.slice_in_dim(x, length - width, length, axis=dim)
        leading = lax.slice_in_dim(x, 0, width, axis=dim)
        before = lax.ppermute(last, axis, up)
        after = lax.ppermute(leading, axis, down)
        x = jnp.concatenate([before, x, after], axis=dim)
    return x


def gelu_exact(values):
    return 0.5 * values * (1.0 + jax.scipy.special.erf(values * inv_root_two))


def gelu_slope(values):
    cdf_part = 0.5 * (1.0 + jax.scipy.special.erf(values * inv_root_two))
    return cdf_part + values * jnp.exp(-0.5 * values * values) * inv_root_two_pi


def body(feature_maps, dw_kernel, norm_gain, w_up, w_down, layer_scale, d_out):
    scenes, strip, across, width = feature_maps.shape
    cells = scenes * strip * across
    hid_axes = ("fsdp", "rows")
    up_loc = lax.all_to_all(w_up, "rows", 1, 0, tiled=True)
    up_loc = lax.all_gather(up_loc, "dp", axis=0, tiled=True)
    down_loc = lax.all_to_all(w_down, "rows", 0, 1, tiled=True)
    down_loc = lax.all_gather(down_loc, "dp", axis=1, tiled=True)
    cotan = d_out.reshape(cells, width).astype(jnp.float32)
    back = (cotan * layer_scale).astype(jnp.bfloat16)
    back_all = lax.all_gather(back, hid_axes, axis=0, tiled=True)
    rimmed = padded_2(feature_maps, (("rows", 1),), 3)
    padded = jnp.pad(rimmed.astype(jnp.float32), ((0, 0), (0, 0), (3, 3), (0, 0)))
    filtered = jnp.zeros(feature_maps.shape, jnp.float32)
    for row_off in range(KS):
        for col_off in range(KS):
            filtered = (
                filtered
                + padded[:, row_off : row_off + strip, col_off : col_off + across, :]
                * dw_kernel[row_off, col_off]
            )
    flat = filtered.reshape(cells, width)
    average = jnp.mean(flat, axis=-1, keepdims=True)
    center = flat - average
    variance = jnp.mean(center * center, axis=-1, keepdims=True)
    rstd = lax.rsqrt(variance + norm_eps)
    normed = center * rstd
    scaled = (normed * norm_gain).astype(jnp.bfloat16)
    gathered = lax.all_gather(scaled, hid_axes, axis=0, tiled=True)
    hidden = jnp.dot(gathered, up_loc, preferred_element_type=jnp.float32)
    active = gelu_exact(hidden).astype(jnp.bfloat16)
    mlp_terms = jnp.dot(active, down_loc, preferred_element_type=jnp.float32)
    branch = lax.psum_scatter(
        mlp_terms.astype(jnp.bfloat16), hid_axes, scatter_dimension=0, tiled=True
    ).astype(jnp.float32)
    resid = feature_maps.reshape(cells, width).astype(jnp.float32)
    result = (resid + layer_scale * branch).astype(jnp.bfloat16).reshape(feature_maps.shape)
    scale_part = jnp.sum(cotan * branch, axis=0)
    down_part = lax.dot_general(active, back_all, contract_rows, preferred_element_type=jnp.float32)
    slope_in = lax.dot_general(
        back_all, down_loc, contract_cols, preferred_element_type=jnp.float32
    )
    hidden_grad = (slope_in * gelu_slope(hidden)).astype(jnp.bfloat16)
    up_part = lax.dot_general(
        gathered, hidden_grad, contract_rows, preferred_element_type=jnp.float32
    )
    norm_terms = lax.dot_general(
        hidden_grad, up_loc, contract_cols, preferred_element_type=jnp.float32
    )
    norm_grad = lax.psum_scatter(norm_terms, hid_axes, scatter_dimension=0, tiled=True)
    grad_up = lax.psum_scatter(up_part, "dp", scatter_dimension=0, tiled=True)
    grad_up = lax.all_to_all(grad_up, "rows", 0, 1, tiled=True)
    grad_down = lax.psum_scatter(down_part, "dp", scatter_dimension=1, tiled=True)
    grad_down = lax.all_to_all(grad_down, "rows", 1, 0, tiled=True)
    gain_part = jnp.sum(norm_grad * normed, axis=0)
    scaled_grad = norm_grad * norm_gain
    conv_grad = rstd * (
        scaled_grad
        - jnp.mean(scaled_grad, axis=-1, keepdims=True)
        - normed * jnp.mean(scaled_grad * normed, axis=-1, keepdims=True)
    )
    conv_grad = conv_grad.reshape(feature_maps.shape)
    grad_rim = padded_2(conv_grad.astype(jnp.bfloat16), (("rows", 1),), 3).astype(conv_grad.dtype)
    grad_pad = jnp.pad(grad_rim, ((0, 0), (0, 0), (3, 3), (0, 0)))
    kernel_rows = []
    back_conv = jnp.zeros(feature_maps.shape, jnp.float32)
    for row_off in range(KS):
        for col_off in range(KS):
            window = padded[:, row_off : row_off + strip, col_off : col_off + across, :]
            kernel_rows.append(jnp.sum(window * conv_grad, axis=(0, 1, 2)))
            back_conv = (
                back_conv
                + grad_pad[
                    :, 6 - row_off : 6 - row_off + strip, 6 - col_off : 6 - col_off + across, :
                ]
                * dw_kernel[row_off, col_off]
            )
    kernel_part = jnp.stack(kernel_rows).reshape(KS, KS, width)
    grad_x = (d_out.astype(jnp.float32) + back_conv).astype(jnp.bfloat16)
    grad_kernel, grad_gain, grad_scale = lax.psum(
        (kernel_part, gain_part, scale_part), ("dp", "fsdp", "rows")
    )
    return (result, grad_x, grad_up, grad_down, grad_kernel, grad_gain, grad_scale)


def solution(mesh):
    return jax.shard_map(
        body,
        mesh=mesh,
        in_specs=(
            P(("dp", "fsdp"), "rows", None, None),
            P(),
            P(),
            P(("dp", "rows"), "fsdp"),
            P("fsdp", ("dp", "rows")),
            P(),
            P(("dp", "fsdp"), "rows", None, None),
        ),
        out_specs=(
            P(("dp", "fsdp"), "rows", None, None),
            P(("dp", "fsdp"), "rows", None, None),
            P(("dp", "rows"), "fsdp"),
            P("fsdp", ("dp", "rows")),
            P(),
            P(),
            P(),
        ),
        check_vma=False,
    )
```

profile of v0, /device:TPU:1, one launch (start us, length us, event | category | flops | bytes accessed | tf_op | source)
XLA Modules:
  0.0 634.2 jit_solution(6933835637550639418)
XLA Ops:
  8.4 13.0 %all_to_all.76 = bf16[96,4,768]{2,0,1:T(8,128)(2,1)} all-to-all(bf16[96,4,768]{2,0,1:T(8,128)(2,1)S(1)} %bitcast.112), channel_id=1, replica_groups=mesh['dp'=4,'fsdp'=2,'rows'=4] {'rows'}, dimensions={1} | all-to-all | bytes 1179648 | tf_op jit(solution)/shard_map/all_to_all | solution.py:41
  27.9 4.3 collective-permute-done.1
  32.4 9.5 %fusion.103 = (f32[4,32]{1,0:T(4,128)S(1)}, f32[1,4,32,1536]{3,2,1,0:T(8,128)S(1)}) fusion(f32[1536]{0:T(1024)S(1)} %get-tuple-element.106, f32[1536]{0:T(1024)S(1)} %get-tuple-element.107, f32[1536]{0:T(1024)S(1)} %get-tuple-element.60, f32[1536]{0:T(1024)S(1)} %get-tuple-element.61, f32[1,10,32,1536]{3,2,1,0:T(8,128)S(1)} %maximum_convert_fusion, ...), kind=kLoop, calls=%fused_computation.315 | loop fusion | flops 19267456 | bytes 8641024 | tf_op jit(solution)/shard_map/reduce_sum | solution.py:59
  44.7 10.7 %all_to_all.77 = bf16[4,768,96]{1,2,0:T(8,128)(2,1)} all-to-all(bf16[4,768,96]{1,2,0:T(8,128)(2,1)S(1)} %bitcast.113), channel_id=1, replica_groups=mesh['dp'=4,'fsdp'=2,'rows'=4] {'rows'}, dimensions={0} | all-to-all | bytes 1179648 | tf_op jit(solution)/shard_map/all_to_all | solution.py:43
  55.5 17.3 %all-gather.7.cloned.1.call-done = bf16[1536,768]{1,0:T(8,128)(2,1)} async-done(((bf16[384,768]{1,0:T(8,128)(2,1)}), bf16[1536,768]{1,0:T(8,128)(2,1)}) %all-gather.7.cloned.1.call-update) | async-done | bytes 2359312 | tf_op jit(solution)/shard_map/all_gather | solution.py:42
  72.8 34.1 %all-gather.5.cloned.1.call-done = bf16[1024,1536]{1,0:T(8,128)(2,1)} async-done(((bf16[128,1536]{1,0:T(8,128)(2,1)}), bf16[1024,1536]{1,0:T(8,128)(2,1)}) %all-gather.5.cloned.1.call-update) | async-done | bytes 3145744 | tf_op jit(solution)/shard_map/all_gather | solution.py:65
  106.9 7.4 %multiply_convert_fusion = (bf16[1024,768]{1,0:T(8,128)(2,1)}, f32[1024,768]{1,0:T(8,128)}) fusion(bf16[1024,1536]{1,0:T(8,128)(2,1)} %all-gather.5.cloned.1.call-done, bf16[1536,768]{1,0:T(8,128)(2,1)} %all-gather.7.cloned.1.call-done), kind=kOutput, calls=%fused_computation.92 | convolution fusion | flops 2419851264 | bytes 10223616 | tf_op jit(solution)/shard_map/dot_general | solution.py:66
  114.3 44.2 %all-gather.9.cloned.1.call-done = bf16[768,1536]{0,1:T(8,128)(2,1)} async-done(((bf16[768,384]{0,1:T(8,128)(2,1)}), bf16[768,1536]{0,1:T(8,128)(2,1)}) %all-gather.9.cloned.1.call-update) | async-done | bytes 2359312 | tf_op jit(solution)/shard_map/all_gather | solution.py:44
  158.5 6.5 %convolution_convert_fusion = bf16[1024,1536]{1,0:T(8,128)(2,1)} fusion(bf16[1024,768]{1,0:T(8,128)(2,1)} %get-tuple-element.120, bf16[768,1536]{0,1:T(8,128)(2,1)} %all-gather.9.cloned.1.call-done), kind=kOutput, calls=%fused_computation.85 | convolution fusion | flops 2417491968 | bytes 7077888 | tf_op jit(solution)/shard_map/dot_general | solution.py:68
  165.1 45.2 %reduce-scatter.5.cloned.1.call-done = bf16[128,1536]{1,0:T(8,128)(2,1)} async-done(((bf16[1024,1536]{1,0:T(8,128)(2,1)}), bf16[128,1536]{1,0:T(8,128)(2,1)}) %reduce-scatter.5.cloned.1.call-update) | async-done | bytes 393232 | tf_op jit(solution)/shard_map/reduce_scatter | solution.py:69
  213.2 32.7 %all-gather.11.cloned.1.call-done = bf16[1024,1536]{1,0:T(8,128)(2,1)} async-done(((bf16[128,1536]{1,0:T(8,128)(2,1)}), bf16[1024,1536]{1,0:T(8,128)(2,1)}) %all-gather.11.cloned.1.call-update) | async-done | bytes 3145744 | tf_op jit(solution)/shard_map/all_gather | solution.py:47
  245.9 7.2 %fusion.108 = f32[768,1536]{1,0:T(8,128)} fusion(bf16[1024,768]{1,0:T(8,128)(2,1)} %get-tuple-element.120, bf16[1024,1536]{1,0:T(8,128)(2,1)} %all-gather.11.cloned.1.call-done), kind=kOutput, calls=%fused_computation.320 | convolution fusion | flops 2415919104 | bytes 9437184 | tf_op jit(solution)/shard_map/dot_general | solution.py:75
  253.1 6.8 %fusion.5 = bf16[1024,768]{1,0:T(8,128)(2,1)S(1)} fusion(f32[1024,768]{1,0:T(8,128)} %get-tuple-element.121, bf16[1024,1536]{1,0:T(8,128)(2,1)} %all-gather.11.cloned.1.call-done, bf16[768,1536]{0,1:T(8,128)(2,1)} %all-gather.9.cloned.1.call-done), kind=kOutput, calls=%fused_computation.91 | convolution fusion | flops 2423783424 | bytes 10223616 | tf_op jit(solution)/shard_map/dot_general | solution.py:76
  261.1 4.6 fusion.106
  265.8 7.2 %fusion.107 = f32[1536,768]{1,0:T(8,128)} fusion(bf16[1024,1536]{1,0:T(8,128)(2,1)} %all-gather.5.cloned.1.call-done, bf16[1024,768]{1,0:T(8,128)(2,1)} %copy-done.49), kind=kOutput, calls=%fused_computation.319 | convolution fusion | flops 2415919104 | bytes 9437184 | tf_op jit(solution)/shard_map/dot_general | solution.py:80
  273.0 65.1 %reduce-scatter.11.cloned.1.call-done = f32[768,384]{1,0:T(8,128)} async-done(((f32[768,1536]{1,0:T(8,128)}), f32[768,384]{1,0:T(8,128)}) %reduce-scatter.11.cloned.1.call-update) | async-done | bytes 1179664 | tf_op jit(solution)/shard_map/reduce_scatter | solution.py:89
  340.8 4.9 all-to-all-start.3
  345.7 58.4 %reduce-scatter.7.cloned.1.call-done = f32[128,1536]{1,0:T(8,128)} async-done(((f32[1024,1536]{1,0:T(8,128)}), f32[128,1536]{1,0:T(8,128)}) %reduce-scatter.7.cloned.1.call-update) | async-done | bytes 786448 | tf_op jit(solution)/shard_map/reduce_scatter | solution.py:86
  431.2 4.2 stack.199
  436.2 46.1 %all-reduce.2 = (f32[1536]{0:T(1024)}, f32[1536]{0:T(1024)}) all-reduce(f32[1536]{0:T(1024)} %get-tuple-element.56, f32[1536]{0:T(1024)} %get-tuple-element.113), channel_id=1, replica_groups=mesh['dp'=4,'fsdp'=2,'rows'=4] {'dp','fsdp','rows'}, use_global_device_ids=true, to_apply=%region_59.60 | all-reduce | flops 3072 | bytes 24576 | tf_op jit(solution)/shard_map/psum | solution.py:116
  482.4 10.4 %reduce-scatter.9.cloned.1.call-done = f32[384,768]{1,0:T(8,128)} async-done(((f32[1536,768]{1,0:T(8,128)}), f32[384,768]{1,0:T(8,128)}) %reduce-scatter.9.cloned.1.call-update) | async-done | bytes 1179664 | tf_op jit(solution)/shard_map/reduce_scatter | solution.py:87
  496.9 8.0 %fusion.96 = bf16[1,4,32,1536]{3,2,1,0:T(8,128)(2,1)} fusion(f32[1,10,32,1536]{3,2,1,0:T(8,128)S(1)} %maximum_convert_fusion.1, bf16[1,4,32,1536]{3,2,1,0:T(8,128)(2,1)S(1)} %copy-done.1, f32[1536]{0:T(1024)} %copy-done.13, f32[1536]{0:T(1024)} %copy-done.14, f32[1536]{0:T(1024)} %copy-done.16, f32[1536]{0:T(1024)} %copy-done.17, f32[1536]{0:T(1024)} %copy-done.18, ...), kind=kLoop, calls=%fused_computation.188 | loop fusion | flops 19660800 | bytes 8562688 | tf_op jit(solution)/shard_map/convert_element_type | solution.py:115
  507.3 5.2 all-to-all-done.2
  513.7 112.3 %all-reduce.5.cloned.1.call-done = f32[7,7,1536]{2,1,0:T(8,128)} async-done(((f32[7,7,1536]{2,1,0:T(8,128)}), f32[7,7,1536]{2,1,0:T(8,128)}) %all-reduce.5.cloned.1.call-update) | async-done | bytes 301072 | tf_op jit(solution)/shard_map/psum | solution.py:116
  (204 shorter events, 54.2 us)
Async XLA Ops:
  7.2 18.9 %copy-start.2 = (f32[7,7,1536]{2,1,0:T(8,128)S(1)}, f32[7,7,1536]{2,1,0:T(8,128)}, u32[]{:S(2)}) copy-start(f32[7,7,1536]{2,1,0:T(8,128)} %param.8) | copy-start | bytes 903172
  7.2 65.6 %all-gather.7.cloned.1.call-start = ((), (), s32[]{:S(2)}) async-start(), calls=%async_computation.9 | async-start | bytes 2949120 | tf_op jit(solution)/shard_map/all_gather | solution.py:42
  21.4 85.5 %all-gather.5.cloned.1.call-start = ((), (), s32[]{:S(2)}) async-start(), calls=%async_computation.8 | async-start | bytes 3538944 | tf_op jit(solution)/shard_map/all_gather | solution.py:65
  21.5 6.3 %collective-permute-start = (bf16[1,3,32,1536]{3,2,1,0:T(8,128)(2,1)S(1)}, bf16[1,3,32,1536]{3,2,1,0:T(8,128)(2,1)S(1)}, u32[]{:S(2)}, u32[]{:S(2)}) collective-permute-start(bf16[1,3,32,1536]{3,2,1,0:T(8,128)(2,1)S(1)} %get-tuple-element.118), channel_id=1, source_target_pairs={{0,1},{1,2},{2,3},{4,5},{5,6},{6,7},{8,9},{9,10},{10,11},{12,13},{... | collective-permute-start | bytes 884744 | tf_op jit(solution)/shard_map/ppermute | solution.py:22
  24.2 8.0 %collective-permute-start.1 = (bf16[1,3,32,1536]{3,2,1,0:T(8,128)(2,1)S(1)}, bf16[1,3,32,1536]{3,2,1,0:T(8,128)(2,1)S(1)}, u32[]{:S(2)}, u32[]{:S(2)}) collective-permute-start(bf16[1,3,32,1536]{3,2,1,0:T(8,128)(2,1)S(1)} %get-tuple-element.119), channel_id=1, source_target_pairs={{1,0},{2,1},{3,2},{5,4},{6,5},{7,6},{9,8},{10,9},{11,10},{13,12},{... | collective-permute-start | bytes 884744 | tf_op jit(solution)/shard_map/ppermute | solution.py:23
  26.3 15.5 %copy-start.4 = (f32[1536]{0:T(1024)}, f32[1536]{0:T(1024)S(1)}, u32[]{:S(2)}) copy-start(f32[1536]{0:T(1024)S(1)} %get-tuple-element.98) | copy-start | bytes 18436
  26.3 15.5 %copy-start.6 = (f32[1536]{0:T(1024)}, f32[1536]{0:T(1024)S(1)}, u32[]{:S(2)}) copy-start(f32[1536]{0:T(1024)S(1)} %get-tuple-element.99) | copy-start | bytes 18436
  26.3 15.5 %copy-start.7 = (f32[1536]{0:T(1024)}, f32[1536]{0:T(1024)S(1)}, u32[]{:S(2)}) copy-start(f32[1536]{0:T(1024)S(1)} %get-tuple-element.100) | copy-start | bytes 18436
  26.3 15.5 %copy-start.8 = (f32[1536]{0:T(1024)}, f32[1536]{0:T(1024)S(1)}, u32[]{:S(2)}) copy-start(f32[1536]{0:T(1024)S(1)} %get-tuple-element.101) | copy-start | bytes 18436
  42.6 71.7 %copy-start.46 = (f32[128]{0:T(128)}, f32[128]{0:T(128)S(1)}, u32[]{:S(2)}) copy-start(f32[128]{0:T(128)S(1)} %rsqrt.12) | copy-start | bytes 1540
  43.6 114.9 %all-gather.9.cloned.1.call-start = ((), (), s32[]{:S(2)}) async-start(), calls=%async_computation.10 | async-start | bytes 2949120 | tf_op jit(solution)/shard_map/all_gather | solution.py:44
  55.4 154.8 %reduce-scatter.5.cloned.1.call-start = ((), (), s32[]{:S(2)}) async-start(), calls=%async_computation.11 | async-start | bytes 3538944 | tf_op jit(solution)/shard_map/reduce_scatter | solution.py:69
  165.0 45.2 %copy-start.1 = (bf16[1,4,32,1536]{3,2,1,0:T(8,128)(2,1)S(1)}, bf16[1,4,32,1536]{3,2,1,0:T(8,128)(2,1)}, u32[]{:S(2)}) copy-start(bf16[1,4,32,1536]{3,2,1,0:T(8,128)(2,1)} %param.13) | copy-start | bytes 1179652
  165.0 80.8 %all-gather.11.cloned.1.call-start = ((), (), s32[]{:S(2)}) async-start(), calls=%async_computation.12 | async-start | bytes 3538944 | tf_op jit(solution)/shard_map/all_gather | solution.py:47
  213.0 125.2 %reduce-scatter.11.cloned.1.call-start = ((), (), s32[]{:S(2)}) async-start(), calls=%async_computation.15 | async-start | bytes 5898240 | tf_op jit(solution)/shard_map/reduce_scatter | solution.py:89
  253.1 151.0 %reduce-scatter.7.cloned.1.call-start = ((), (), s32[]{:S(2)}) async-start(), calls=%async_computation.13 | async-start | bytes 7077888 | tf_op jit(solution)/shard_map/reduce_scatter | solution.py:86
  265.7 227.1 %reduce-scatter.9.cloned.1.call-start = ((), (), s32[]{:S(2)}) async-start(), calls=%async_computation.14 | async-start | bytes 5898240 | tf_op jit(solution)/shard_map/reduce_scatter | solution.py:87
  273.0 131.1 %copy-start.45 = (f32[128]{0:T(128)S(1)}, f32[128]{0:T(128)}, u32[]{:S(2)}) copy-start(f32[128]{0:T(128)} %copy-done.44) | copy-start | bytes 1540
  273.0 131.1 %copy-start.47 = (f32[128]{0:T(128)S(1)}, f32[128]{0:T(128)}, u32[]{:S(2)}) copy-start(f32[128]{0:T(128)} %copy-done.46) | copy-start | bytes 1540
  340.8 152.0 %all-to-all-start.3 = ((f32[768,4,96]{0,2,1:T(8,128)}), f32[768,4,96]{0,2,1:T(8,128)}, u32[]{:S(2)}, u32[]{:S(2)}) async-start(f32[768,4,96]{0,2,1:T(8,128)} %bitcast.108), calls=%async_computation.7 | async-start | bytes 2359296 | tf_op jit(solution)/shard_map/all_to_all | solution.py:90
  345.7 280.3 %all-reduce.5.cloned.1.call-start = ((), (), s32[]{:S(2)}) async-start(), calls=%async_computation.16 | async-start | bytes 688128 | tf_op jit(solution)/shard_map/psum | solution.py:116
  424.1 58.2 %collective-permute-start.2 = (bf16[1,3,32,1536]{3,2,1,0:T(8,128)(2,1)}, bf16[1,3,32,1536]{3,2,1,0:T(8,128)(2,1)S(1)}, u32[]{:S(2)}, u32[]{:S(2)}) collective-permute-start(bf16[1,3,32,1536]{3,2,1,0:T(8,128)(2,1)} %get-tuple-element.116), channel_id=1, source_target_pairs={{0,1},{1,2},{2,3},{4,5},{5,6},{6,7},{8,9},{9,10},{10,11},{12,13},{... | collective-permute-start | bytes 884744 | tf_op jit(solution)/shard_map/ppermute | solution.py:22
  427.7 54.6 %collective-permute-start.3 = (bf16[1,3,32,1536]{3,2,1,0:T(8,128)(2,1)}, bf16[1,3,32,1536]{3,2,1,0:T(8,128)(2,1)S(1)}, u32[]{:S(2)}, u32[]{:S(2)}) collective-permute-start(bf16[1,3,32,1536]{3,2,1,0:T(8,128)(2,1)} %get-tuple-element.117), channel_id=1, source_target_pairs={{1,0},{2,1},{3,2},{5,4},{6,5},{7,6},{9,8},{10,9},{11,10},{13,12},{... | collective-permute-start | bytes 884744 | tf_op jit(solution)/shard_map/ppermute | solution.py:23
  492.8 19.8 %all-to-all-start.2 = ((f32[4,96,768]{2,1,0:T(8,128)}), f32[4,96,768]{2,1,0:T(8,128)S(1)}, u32[]{:S(2)}, u32[]{:S(2)}) async-start(f32[4,96,768]{2,1,0:T(8,128)} %bitcast.115), calls=%async_computation.5 | async-start | bytes 2359296 | tf_op jit(solution)/shard_map/all_to_all | solution.py:88
  (41 other events, 586.9 us)
Sparse Core Ops, SparseCore 0:
  21.5 51.2 all-gather.6
  75.3 31.5 all-gather.4
  108.5 50.0 all-gather.8
  165.1 45.0 reduce-scatter.4
  213.1 32.7 all-gather.10
  253.2 84.8 reduce-scatter.10
  341.9 62.1 reduce-scatter.6
  406.4 86.3 reduce-scatter.8
  498.7 127.2 all-reduce.4
where the time goes:
time: 635 us; the launch traced here: 634 us
  waiting for transfers between devices  429 us (68%)
  blocking collectives  69.8 us (11%)
  matrix products  39.7 us (6%)
  local copies, waits for them, and re-layouts  30.5 us (5%)
  other arithmetic  30.4 us (5%)
  starting transfers between devices  19.6 us (3%)
  between operations  14.9 us (2%)
    psum x1, waiting for transfers between devices, body(): lax.psum((kernel_part, gain_part, scale_part), ('dp', 'fsdp', 'rows'))  112 us
    reduce_scatter x1, waiting for transfers between devices, body(): lax.psum_scatter(down_part, 'dp', scatter_dimension=1, tiled=True)  65.1 us
    reduce_scatter x1, waiting for transfers between devices, body(): lax.psum_scatter(norm_terms, hid_axes, scatter_dimension=0, tiled=True)  58.4 us
    psum x1, blocking collectives, body(): lax.psum((kernel_part, gain_part, scale_part), ('dp', 'fsdp', 'rows'))  46.1 us
    reduce_scatter x1, waiting for transfers between devices, body(): lax.psum_scatter(mlp_terms.astype(jnp.bfloat16), hid_axes, scatter_dimens...  45.2 us
    all_gather x1, waiting for transfers between devices, body(): down_loc = lax.all_gather(down_loc, 'dp', axis=1, tiled=True)  44.2 us
    all_gather x1, waiting for transfers between devices, body(): gathered = lax.all_gather(scaled, hid_axes, axis=0, tiled=True)  34.1 us
    all_gather x1, waiting for transfers between devices, body(): back_all = lax.all_gather(back, hid_axes, axis=0, tiled=True)  32.7 us
  transfers between devices with their start and end apart: 15, of which 11 were waited for; matrix products, arithmetic and copies ran while one was open for 13% of the time, Pallas kernels for 0%

commit v1 on v0

--- a/solution.py
+++ b/solution.py
@@ -41,7 +41,16 @@
     up_loc = lax.all_to_all(w_up, "rows", 1, 0, tiled=True)
     up_loc = lax.all_gather(up_loc, "dp", axis=0, tiled=True)
     down_loc = lax.all_to_all(w_down, "rows", 0, 1, tiled=True)
-    down_loc = lax.all_gather(down_loc, "dp", axis=1, tiled=True)
+    ways = lax.axis_size("dp")
+    up_2 = [(d, (d + 1) % ways) for d in range(ways)]
+    down_2 = [(d, (d - 1) % ways) for d in range(ways)]
+    earlier, later = ([down_loc], [down_loc])
+    for _ in range(ways // 2):
+        earlier.append(lax.ppermute(earlier[-1], "dp", up_2))
+    for _ in range((ways - 1) // 2):
+        later.append(lax.ppermute(later[-1], "dp", down_2))
+    line = jnp.concatenate([*earlier[::-1], *later[1:]], axis=1)
+    down_loc = jnp.roll(line, (lax.axis_index("dp") - ways // 2) * down_loc.shape[1], axis=1)
     cotan = d_out.reshape(cells, width).astype(jnp.float32)
     back = (cotan * layer_scale).astype(jnp.bfloat16)
     back_all = lax.all_gather(back, hid_axes, axis=0, tiled=True)

time: 635 us -> 607 us (0.956)
  waiting for transfers between devices: 429 us -> 382 us
  local copies, waits for them, and re-layouts: 30.5 us -> 42.8 us
    ppermute x0 -> x3, waiting for transfers between devices: none -> 47.4 us  [the longest x2 41.5 us: body(): earlier.append(lax.ppermute(earlier[-1], 'dp', up_2))]
    all_gather x1 -> x0, waiting for transfers between devices: 44.2 us -> none  [body(): down_loc = lax.all_gather(down_loc, 'dp', axis=1, tiled=True)]
    all_gather x1, waiting for transfers between devices: 34.1 us -> 0.01 us  [body(): gathered = lax.all_gather(scaled, hid_axes, axis=0, tiled=True)]
    all_gather x1, waiting for transfers between devices: 17.3 us -> 0.01 us  [body(): up_loc = lax.all_gather(up_loc, 'dp', axis=0, tiled=True)]
    unnamed x101 -> x112, local copies, waits for them, and re-layouts: 3.09 us -> 14.5 us
  transfers between devices with their start and end apart: 15 -> 17, of which waited for: 11 -> 11; matrix products, arithmetic and copies ran while one was open for 13% -> 14% of each run, Pallas kernels for 0% -> 0%
where the time goes in v1:
time: 607 us; the launch traced here: 605 us
  waiting for transfers between devices  382 us (63%)
  blocking collectives  69.8 us (11%)
  local copies, waits for them, and re-layouts  42.8 us (7%)
  matrix products  39.9 us (7%)
  other arithmetic  31.4 us (5%)
  starting transfers between devices  24.5 us (4%)
  between operations  15.2 us (3%)
    psum x1, waiting for transfers between devices, body(): lax.psum((kernel_part, gain_part, scale_part), ('dp', 'fsdp', 'rows'))  112 us
    reduce_scatter x1, waiting for transfers between devices, body(): lax.psum_scatter(down_part, 'dp', scatter_dimension=1, tiled=True)  64.9 us
    reduce_scatter x1, waiting for transfers between devices, body(): lax.psum_scatter(norm_terms, hid_axes, scatter_dimension=0, tiled=True)  58.3 us
    reduce_scatter x1, waiting for transfers between devices, body(): lax.psum_scatter(mlp_terms.astype(jnp.bfloat16), hid_axes, scatter_dimens...  47.1 us
    psum x1, blocking collectives, body(): lax.psum((kernel_part, gain_part, scale_part), ('dp', 'fsdp', 'rows'))  46.1 us
    ppermute x2, waiting for transfers between devices, body(): earlier.append(lax.ppermute(earlier[-1], 'dp', up_2))  41.5 us
    all_gather x1, waiting for transfers between devices, body(): back_all = lax.all_gather(back, hid_axes, axis=0, tiled=True)  32.6 us
    another operation x50, local copies, waits for them, and re-layouts, body(): kernel_part = jnp.stack(kernel_rows).reshape(KS, KS, width)  15.7 us
  transfers between devices with their start and end apart: 17, of which 11 were waited for; matrix products, arithmetic and copies ran while one was open for 14% of the time, Pallas kernels for 0%

profile of v1, /device:TPU:1, one launch (start us, length us, event | category | flops | bytes accessed | tf_op | source)
XLA Modules:
  0.0 605.3 jit_solution(11796747628798982255)
XLA Ops:
  8.4 13.0 %all_to_all.76 = bf16[96,4,768]{2,0,1:T(8,128)(2,1)} all-to-all(bf16[96,4,768]{2,0,1:T(8,128)(2,1)S(1)} %bitcast.113), channel_id=1, replica_groups=mesh['dp'=4,'fsdp'=2,'rows'=4] {'rows'}, dimensions={1} | all-to-all | bytes 1179648 | tf_op jit(solution)/shard_map/all_to_all | solution.py:41
  27.9 4.3 collective-permute-done.1
  32.8 9.4 %fusion.110 = (f32[4,32]{1,0:T(4,128)S(1)}, f32[1,4,32,1536]{3,2,1,0:T(8,128)S(1)}) fusion(f32[1536]{0:T(1024)S(1)} %get-tuple-element.106, f32[1536]{0:T(1024)S(1)} %get-tuple-element.107, f32[1536]{0:T(1024)S(1)} %get-tuple-element.60, f32[1536]{0:T(1024)S(1)} %get-tuple-element.61, f32[1,10,32,1536]{3,2,1,0:T(8,128)S(1)} %maximum_convert_fusion, ...), kind=kLoop, calls=%fused_computation.328 | loop fusion | flops 19267456 | bytes 8641024 | tf_op jit(solution)/shard_map/reduce_sum | solution.py:68
  43.7 10.7 %all_to_all.77 = bf16[4,768,96]{1,2,0:T(8,128)(2,1)S(1)} all-to-all(bf16[4,768,96]{1,2,0:T(8,128)(2,1)S(1)} %bitcast.114), channel_id=1, replica_groups=mesh['dp'=4,'fsdp'=2,'rows'=4] {'rows'}, dimensions={0} | all-to-all | bytes 1179648 | tf_op jit(solution)/shard_map/all_to_all | solution.py:43
  56.1 28.8 %collective-permute-done.2 = bf16[768,384]{0,1:T(8,128)(2,1)} collective-permute-done((bf16[768,384]{0,1:T(8,128)(2,1)S(1)}, bf16[768,384]{0,1:T(8,128)(2,1)}, u32[]{:S(2)}, u32[]{:S(2)}) %collective-permute-start.2) | collective-permute-done | bytes 589856 | tf_op jit(solution)/shard_map/ppermute | solution.py:49
  88.1 12.7 %collective-permute-done.3 = bf16[768,384]{0,1:T(8,128)(2,1)} collective-permute-done((bf16[768,384]{0,1:T(8,128)(2,1)}, bf16[768,384]{0,1:T(8,128)(2,1)}, u32[]{:S(2)}, u32[]{:S(2)}) %collective-permute-start.3) | collective-permute-done | bytes 589856 | tf_op jit(solution)/shard_map/ppermute | solution.py:49
  105.6 5.8 collective-permute-done.4
  120.0 7.4 %multiply_convert_fusion = (bf16[1024,768]{1,0:T(8,128)(2,1)}, f32[1024,768]{1,0:T(8,128)}) fusion(bf16[1024,1536]{1,0:T(8,128)(2,1)} %all-gather.4.cloned.1.call-done, bf16[1536,768]{1,0:T(8,128)(2,1)} %all-gather.6.cloned.1.call-done), kind=kOutput, calls=%fused_computation.92 | convolution fusion | flops 2419851264 | bytes 10223616 | tf_op jit(solution)/shard_map/dot_general | solution.py:75
  127.4 6.5 %convolution_convert_fusion = bf16[1024,1536]{1,0:T(8,128)(2,1)} fusion(bf16[1024,768]{1,0:T(8,128)(2,1)} %get-tuple-element.120, bf16[768,3072]{0,1:T(8,128)(2,1)} %constant_dynamic-update-slice_fusion, s32[]{:T(128)S(6)} %select_n.14), kind=kOutput, calls=%fused_computation.85 | convolution fusion | flops 2417491968 | bytes 7077892 | tf_op jit(solution)/shard_map/dot_general | solution.py:77
  134.0 47.1 %reduce-scatter.5.cloned.1.call-done = bf16[128,1536]{1,0:T(8,128)(2,1)} async-done(((bf16[1024,1536]{1,0:T(8,128)(2,1)}), bf16[128,1536]{1,0:T(8,128)(2,1)}) %reduce-scatter.5.cloned.1.call-update) | async-done | bytes 393232 | tf_op jit(solution)/shard_map/reduce_scatter | solution.py:78
  184.1 32.6 %all-gather.8.cloned.1.call-done = bf16[1024,1536]{1,0:T(8,128)(2,1)} async-done(((bf16[128,1536]{1,0:T(8,128)(2,1)}), bf16[1024,1536]{1,0:T(8,128)(2,1)}) %all-gather.8.cloned.1.call-update) | async-done | bytes 3145744 | tf_op jit(solution)/shard_map/all_gather | solution.py:56
  216.8 7.2 %fusion.115 = f32[768,1536]{1,0:T(8,128)} fusion(bf16[1024,768]{1,0:T(8,128)(2,1)} %get-tuple-element.120, bf16[1024,1536]{1,0:T(8,128)(2,1)} %all-gather.8.cloned.1.call-done), kind=kOutput, calls=%fused_computation.333 | convolution fusion | flops 2415919104 | bytes 9437184 | tf_op jit(solution)/shard_map/dot_general | solution.py:84
  224.1 6.9 %fusion.5 = bf16[1024,768]{1,0:T(8,128)(2,1)S(1)} fusion(f32[1024,768]{1,0:T(8,128)} %get-tuple-element.121, bf16[1024,1536]{1,0:T(8,128)(2,1)} %all-gather.8.cloned.1.call-done, bf16[768,3072]{0,1:T(8,128)(2,1)} %constant_dynamic-update-slice_fusion, s32[]{:T(128)S(6)} %select_n.14), kind=kOutput, calls=%fused_computation.91 | convolution fusion | flops 2423783424 | bytes 10223620 | tf_op jit(solution)/shard_map/dot_general | solution.py:85
  232.2 4.6 fusion.113
  236.8 7.2 %fusion.114 = f32[1536,768]{1,0:T(8,128)} fusion(bf16[1024,1536]{1,0:T(8,128)(2,1)} %all-gather.4.cloned.1.call-done, bf16[1024,768]{1,0:T(8,128)(2,1)} %copy-done.51), kind=kOutput, calls=%fused_computation.332 | convolution fusion | flops 2415919104 | bytes 9437184 | tf_op jit(solution)/shard_map/dot_general | solution.py:89
  244.1 64.9 %reduce-scatter.11.cloned.1.call-done = f32[768,384]{1,0:T(8,128)} async-done(((f32[768,1536]{1,0:T(8,128)}), f32[768,384]{1,0:T(8,128)}) %reduce-scatter.11.cloned.1.call-update) | async-done | bytes 1179664 | tf_op jit(solution)/shard_map/reduce_scatter | solution.py:98
  311.7 4.9 all-to-all-start.3
  316.6 58.3 %reduce-scatter.7.cloned.1.call-done = f32[128,1536]{1,0:T(8,128)} async-done(((f32[1024,1536]{1,0:T(8,128)}), f32[128,1536]{1,0:T(8,128)}) %reduce-scatter.7.cloned.1.call-update) | async-done | bytes 786448 | tf_op jit(solution)/shard_map/reduce_scatter | solution.py:95
  402.0 4.2 stack.199
  406.9 46.1 %all-reduce.2 = (f32[1536]{0:T(1024)}, f32[1536]{0:T(1024)}) all-reduce(f32[1536]{0:T(1024)} %get-tuple-element.56, f32[1536]{0:T(1024)} %get-tuple-element.113), channel_id=1, replica_groups=mesh['dp'=4,'fsdp'=2,'rows'=4] {'dp','fsdp','rows'}, use_global_device_ids=true, to_apply=%region_59.60 | all-reduce | flops 3072 | bytes 24576 | tf_op jit(solution)/shard_map/psum | solution.py:125
  454.2 9.4 %reduce-scatter.9.cloned.1.call-done = f32[384,768]{1,0:T(8,128)} async-done(((f32[1536,768]{1,0:T(8,128)}), f32[384,768]{1,0:T(8,128)}) %reduce-scatter.9.cloned.1.call-update) | async-done | bytes 1179664 | tf_op jit(solution)/shard_map/reduce_scatter | solution.py:96
  467.7 8.0 %fusion.101 = bf16[1,4,32,1536]{3,2,1,0:T(8,128)(2,1)} fusion(f32[1,10,32,1536]{3,2,1,0:T(8,128)S(1)} %maximum_convert_fusion.1, bf16[1,4,32,1536]{3,2,1,0:T(8,128)(2,1)S(1)} %copy-done.2, f32[1536]{0:T(1024)} %copy-done.15, f32[1536]{0:T(1024)} %copy-done.16, f32[1536]{0:T(1024)} %copy-done.18, f32[1536]{0:T(1024)} %copy-done.19, f32[1536]{0:T(1024)} %copy-done.20, ...), kind=kLoop, calls=%fused_computation.191 | loop fusion | flops 19660800 | bytes 8562688 | tf_op jit(solution)/shard_map/convert_element_type | solution.py:124
  478.1 5.2 all-to-all-done.2
  484.4 112.2 %all-reduce.5.cloned.1.call-done = f32[7,7,1536]{2,1,0:T(8,128)} async-done(((f32[7,7,1536]{2,1,0:T(8,128)}), f32[7,7,1536]{2,1,0:T(8,128)}) %all-reduce.5.cloned.1.call-update) | async-done | bytes 301072 | tf_op jit(solution)/shard_map/psum | solution.py:125
  (219 shorter events, 72.4 us)
Async XLA Ops:
  7.2 18.9 %copy-start.4 = (f32[7,7,1536]{2,1,0:T(8,128)S(1)}, f32[7,7,1536]{2,1,0:T(8,128)}, u32[]{:S(2)}) copy-start(f32[7,7,1536]{2,1,0:T(8,128)} %param.8) | copy-start | bytes 903172
  7.2 112.8 %all-gather.6.cloned.1.call-start = ((), (), s32[]{:S(2)}) async-start(), calls=%async_computation.9 | async-start | bytes 2949120 | tf_op jit(solution)/shard_map/all_gather | solution.py:42
  21.4 98.6 %all-gather.4.cloned.1.call-start = ((), (), s32[]{:S(2)}) async-start(), calls=%async_computation.8 | async-start | bytes 3538944 | tf_op jit(solution)/shard_map/all_gather | solution.py:74
  21.5 6.3 %collective-permute-start = (bf16[1,3,32,1536]{3,2,1,0:T(8,128)(2,1)S(1)}, bf16[1,3,32,1536]{3,2,1,0:T(8,128)(2,1)S(1)}, u32[]{:S(2)}, u32[]{:S(2)}) collective-permute-start(bf16[1,3,32,1536]{3,2,1,0:T(8,128)(2,1)S(1)} %get-tuple-element.118), channel_id=1, source_target_pairs={{0,1},{1,2},{2,3},{4,5},{5,6},{6,7},{8,9},{9,10},{10,11},{12,13},{... | collective-permute-start | bytes 884744 | tf_op jit(solution)/shard_map/ppermute | solution.py:22
  24.2 8.0 %collective-permute-start.1 = (bf16[1,3,32,1536]{3,2,1,0:T(8,128)(2,1)S(1)}, bf16[1,3,32,1536]{3,2,1,0:T(8,128)(2,1)S(1)}, u32[]{:S(2)}, u32[]{:S(2)}) collective-permute-start(bf16[1,3,32,1536]{3,2,1,0:T(8,128)(2,1)S(1)} %get-tuple-element.119), channel_id=1, source_target_pairs={{1,0},{2,1},{3,2},{5,4},{6,5},{7,6},{9,8},{10,9},{11,10},{13,12},{... | collective-permute-start | bytes 884744 | tf_op jit(solution)/shard_map/ppermute | solution.py:23
  42.3 60.5 %copy-start.46 = (f32[128]{0:T(128)}, f32[128]{0:T(128)S(1)}, u32[]{:S(2)}) copy-start(f32[128]{0:T(128)S(1)} %div.15) | copy-start | bytes 1540
  42.6 60.2 %copy-start.48 = (f32[128]{0:T(128)}, f32[128]{0:T(128)S(1)}, u32[]{:S(2)}) copy-start(f32[128]{0:T(128)S(1)} %rsqrt.12) | copy-start | bytes 1540
  43.6 137.6 %reduce-scatter.5.cloned.1.call-start = ((), (), s32[]{:S(2)}) async-start(), calls=%async_computation.10 | async-start | bytes 3538944 | tf_op jit(solution)/shard_map/reduce_scatter | solution.py:78
  54.4 30.5 %collective-permute-start.2 = (bf16[768,384]{0,1:T(8,128)(2,1)S(1)}, bf16[768,384]{0,1:T(8,128)(2,1)}, u32[]{:S(2)}, u32[]{:S(2)}) collective-permute-start(bf16[768,384]{0,1:T(8,128)(2,1)S(1)} %bitcast.106), channel_id=1, source_target_pairs={{0,8},{8,16},{16,24},{24,0},{1,9},{9,17},{17,25},{25,1},{2,10},{10... | collective-permute-start | bytes 1769480 | tf_op jit(solution)/shard_map/ppermute | solution.py:49
  84.9 16.0 %collective-permute-start.3 = (bf16[768,384]{0,1:T(8,128)(2,1)}, bf16[768,384]{0,1:T(8,128)(2,1)}, u32[]{:S(2)}, u32[]{:S(2)}) collective-permute-start(bf16[768,384]{0,1:T(8,128)(2,1)} %collective-permute-done.2), channel_id=1, source_target_pairs={{0,8},{8,16},{16,24},{24,0},{1,9},{9,17},{17,25},{25,1},{2,10},{10... | collective-permute-start | bytes 1769480 | tf_op jit(solution)/shard_map/ppermute | solution.py:49
  84.9 26.5 %collective-permute-start.4 = (bf16[768,384]{0,1:T(8,128)(2,1)S(1)}, bf16[768,384]{0,1:T(8,128)(2,1)}, u32[]{:S(2)}, u32[]{:S(2)}) collective-permute-start(bf16[768,384]{0,1:T(8,128)(2,1)S(1)} %bitcast.107), channel_id=1, source_target_pairs={{0,24},{8,0},{16,8},{24,16},{1,25},{9,1},{17,9},{25,17},{2,26},{10... | collective-permute-start | bytes 1769480 | tf_op jit(solution)/shard_map/ppermute | solution.py:51
  134.0 47.2 %copy-start.1 = (bf16[1,4,32,1536]{3,2,1,0:T(8,128)(2,1)S(1)}, bf16[1,4,32,1536]{3,2,1,0:T(8,128)(2,1)}, u32[]{:S(2)}) copy-start(bf16[1,4,32,1536]{3,2,1,0:T(8,128)(2,1)} %param.7) | copy-start | bytes 1179652
  134.0 47.2 %copy-start.2 = (bf16[1,4,32,1536]{3,2,1,0:T(8,128)(2,1)S(1)}, bf16[1,4,32,1536]{3,2,1,0:T(8,128)(2,1)}, u32[]{:S(2)}) copy-start(bf16[1,4,32,1536]{3,2,1,0:T(8,128)(2,1)} %param.13) | copy-start | bytes 1179652
  134.0 82.8 %all-gather.8.cloned.1.call-start = ((), (), s32[]{:S(2)}) async-start(), calls=%async_computation.11 | async-start | bytes 3538944 | tf_op jit(solution)/shard_map/all_gather | solution.py:56
  183.9 125.2 %reduce-scatter.11.cloned.1.call-start = ((), (), s32[]{:S(2)}) async-start(), calls=%async_computation.14 | async-start | bytes 5898240 | tf_op jit(solution)/shard_map/reduce_scatter | solution.py:98
  224.0 150.9 %reduce-scatter.7.cloned.1.call-start = ((), (), s32[]{:S(2)}) async-start(), calls=%async_computation.12 | async-start | bytes 7077888 | tf_op jit(solution)/shard_map/reduce_scatter | solution.py:95
  236.8 226.8 %reduce-scatter.9.cloned.1.call-start = ((), (), s32[]{:S(2)}) async-start(), calls=%async_computation.13 | async-start | bytes 5898240 | tf_op jit(solution)/shard_map/reduce_scatter | solution.py:96
  244.1 130.8 %copy-start.47 = (f32[128]{0:T(128)S(1)}, f32[128]{0:T(128)}, u32[]{:S(2)}) copy-start(f32[128]{0:T(128)} %copy-done.46) | copy-start | bytes 1540
  244.1 130.8 %copy-start.49 = (f32[128]{0:T(128)S(1)}, f32[128]{0:T(128)}, u32[]{:S(2)}) copy-start(f32[128]{0:T(128)} %copy-done.48) | copy-start | bytes 1540
  311.7 151.8 %all-to-all-start.3 = ((f32[768,4,96]{0,2,1:T(8,128)}), f32[768,4,96]{0,2,1:T(8,128)}, u32[]{:S(2)}, u32[]{:S(2)}) async-start(f32[768,4,96]{0,2,1:T(8,128)} %bitcast.110), calls=%async_computation.7 | async-start | bytes 2359296 | tf_op jit(solution)/shard_map/all_to_all | solution.py:99
  316.6 280.1 %all-reduce.5.cloned.1.call-start = ((), (), s32[]{:S(2)}) async-start(), calls=%async_computation.15 | async-start | bytes 688128 | tf_op jit(solution)/shard_map/psum | solution.py:125
  394.8 58.2 %collective-permute-start.5 = (bf16[1,3,32,1536]{3,2,1,0:T(8,128)(2,1)}, bf16[1,3,32,1536]{3,2,1,0:T(8,128)(2,1)S(1)}, u32[]{:S(2)}, u32[]{:S(2)}) collective-permute-start(bf16[1,3,32,1536]{3,2,1,0:T(8,128)(2,1)} %get-tuple-element.116), channel_id=1, source_target_pairs={{0,1},{1,2},{2,3},{4,5},{5,6},{6,7},{8,9},{9,10},{10,11},{12,13},{... | collective-permute-start | bytes 884744 | tf_op jit(solution)/shard_map/ppermute | solution.py:22
  398.4 54.6 %collective-permute-start.6 = (bf16[1,3,32,1536]{3,2,1,0:T(8,128)(2,1)}, bf16[1,3,32,1536]{3,2,1,0:T(8,128)(2,1)}, u32[]{:S(2)}, u32[]{:S(2)}) collective-permute-start(bf16[1,3,32,1536]{3,2,1,0:T(8,128)(2,1)} %get-tuple-element.117), channel_id=1, source_target_pairs={{1,0},{2,1},{3,2},{5,4},{6,5},{7,6},{9,8},{10,9},{11,10},{13,12},{... | collective-permute-start | bytes 884744 | tf_op jit(solution)/shard_map/ppermute | solution.py:23
  463.6 19.8 %all-to-all-start.2 = ((f32[4,96,768]{2,1,0:T(8,128)}), f32[4,96,768]{2,1,0:T(8,128)S(1)}, u32[]{:S(2)}, u32[]{:S(2)}) async-start(f32[4,96,768]{2,1,0:T(8,128)} %bitcast.116), calls=%async_computation.5 | async-start | bytes 2359296 | tf_op jit(solution)/shard_map/all_to_all | solution.py:97
  (45 other events, 268.1 us)
Sparse Core Ops, SparseCore 0:
  21.5 63.6 all-gather.5
  87.7 31.6 all-gather.3
  134.1 47.0 reduce-scatter.4
  184.0 32.7 all-gather.7
  224.1 84.8 reduce-scatter.10
  312.7 62.1 reduce-scatter.6
  377.2 86.3 reduce-scatter.8
  469.5 127.1 all-reduce.4
